TPU v7x, 32 devices: a whole 2x2x4 slice. The times are simulated.
32 devices in a mesh: dp: 4 (over y, x), expert: 8 (over z, core).
Axes of the slice: x: 2, y: 2, z: 4, core: 2. Of those that a mesh axis runs over, the one named last changes fastest.
Arguments:
- hidden: bfloat16 [32, 2048], P(('dp', 'expert')), may hold values from -6 to 6
- attn_gain: float32 [2048], replicated, may hold values from 0.25 to 1.75
- query_weight: bfloat16 [3072, 2048], P('expert'), may hold values from -0.125 to 0.125
- latent_down: bfloat16 [2048, 576], replicated, may hold values from -0.125 to 0.125
- latent_up: bfloat16 [512, 4096], P(None, 'expert'), may hold values from -0.25 to 0.25
- out_weight: bfloat16 [2048, 2048], P('expert'), may hold values from -0.125 to 0.125
- latent_pool: bfloat16 [128, 32, 576], P('dp'), may hold values from -1000 to 1000
- page_table: int32 [32, 16], replicated, may hold values from -1 to 127, as said below
- page_counts: int32 [32], replicated, may hold values from 1 to 16, as said below
- ffn_gain: float32 [2048], replicated, may hold values from 0.25 to 1.75
- expert_ids: int32 [32, 6], replicated, may hold values from 0 to 23, all different within a row; in each aligned block of 32 rows (0 to 31, 32 to 63, ...) at most 16 rows name the same one
- expert_gates: float32 [32, 6], replicated, may hold values from 0.05 to 0.6
- old_place: int32 [8, 4], replicated, may hold values from 0 to 23, as said below
- new_place: int32 [8, 4], replicated, may hold values from 0 to 23, as said below
- expert_gate_up: bfloat16 [32, 2, 1408, 2048], P('expert', None, None, 'dp'), as said below
- expert_down: bfloat16 [32, 1408, 2048], P('expert', None, 'dp'), as said below
- shared_gate_up: bfloat16 [2, 2816, 2048], P(None, None, 'dp'), may hold values from -0.125 to 0.125
- shared_down: bfloat16 [2816, 2048], P(None, 'dp'), may hold values from -0.109375 to 0.109375
Outputs:
- layer_out: bfloat16 [32, 2048], P(('dp', 'expert'))
- moved_gate_up: bfloat16 [32, 2, 1408, 2048], P('expert', None, None, 'dp')
- moved_down: bfloat16 [32, 1408, 2048], P('expert', None, 'dp')
Inputs may be any that keep to these rules, and one draw needn't show every extreme that they name: `page_counts`: each request's count of cached pages; exactly one request has 16. `page_table`: row t names page_counts[t] pages of the pool, no page named twice in the table; its other entries are -1. Page p lies on dp index p // 32. `expert_ids`: no expert is named by more than 16 tokens in all; some expert by exactly 16. `old_place`: row i holds the experts of the slots on expert index i, slot s of row i being global slot i * 4 + s; every expert is held by one slot or more. `new_place`: equal to old_place except in exactly one slot of each row, which names another expert. `expert_gate_up`: slots that hold the same expert under old_place hold equal weights. `expert_down`: slots that hold the same expert under old_place hold equal weights.
All inputs are finite; a program needn't handle non-finite values.
Results may differ from a plain program's by a relative error of at most 0.02.
Values may be sent and summed in bfloat16 or wider, within the bound.
No kernel may reach another device: no remote copies, remote signals or barrier semaphores. Data moves between devices by JAX's collectives and lax.ppermute only.
A program may use at most 128 MiB of HBM per device.

v0:
```python
import math
import jax
import jax.numpy as jnp
from jax import lax
from jax.sharding import PartitionSpec as P

NOPE = 128
ROPE = 64
VHEAD = 128
LATENT = 512
EXP_DEV = 3
PAGE = 32
EPSILON = 1e-06
ROPE_BASE = 50000.0
MASKED_SCORE = -1e30
HIGHEST = lax.Precision.HIGHEST


def rms_plain(values):
    mean_square = jnp.mean(values * values, axis=-1, keepdims=True)
    return values * lax.rsqrt(mean_square + EPSILON)


def rms_norm(values, norm_gain):
    return rms_plain(values) * norm_gain


def rotary(values, position):
    half_width = values.shape[-1] // 2
    exponent = jnp.arange(half_width).astype(jnp.float32) * (2.0 / values.shape[-1])
    frequency = jnp.exp(-exponent * math.log(ROPE_BASE))
    angles = position[..., None] * frequency
    cosine = jnp.cos(angles)
    sine_part = jnp.sin(angles)
    first_half = values[..., :half_width]
    second = values[..., half_width:]
    return jnp.concatenate(
        [first_half * cosine - second * sine_part, second * cosine + first_half * sine_part],
        axis=-1,
    )


def gather_rows(rows):
    by_expert = lax.all_gather(rows, "expert", axis=0, tiled=True)
    return lax.all_gather(by_expert, "dp", axis=0, tiled=True)


def spread_slots(gate_up, down, picks, ex_count):
    chosen = jnp.concatenate([gate_up[picks], down[picks][:, None]], axis=1)
    count, parts, ff_width, col_width = chosen.shape
    pieces = chosen.reshape(count, parts, ex_count, ff_width // ex_count, col_width)
    spread = lax.all_to_all(pieces, "expert", split_axis=2, concat_axis=0, tiled=True)
    return spread.reshape(ex_count * count, parts, ff_width // ex_count, col_width)


def migrate(expert_gate_up, expert_down, old_place, new_place, ex_index):
    rows, slots_local = old_place.shape
    slots = rows * slots_local
    ex_count = rows
    ff_width = expert_gate_up.shape[2]
    changed = old_place != new_place
    moved_slot = jnp.argmax(changed, axis=1)
    wanted = jnp.take_along_axis(new_place, moved_slot[:, None], axis=1)[:, 0]
    hit = old_place.reshape(-1)[None, :] == wanted[:, None]
    first = jnp.argmax(hit, axis=1).astype(jnp.int32)
    last = (slots - 1 - jnp.argmax(hit[:, ::-1], axis=1)).astype(jnp.int32)
    slot_ids = jnp.arange(slots, dtype=jnp.int32)

    def needed_of(src):
        needed = jnp.any(src[:, None] == slot_ids[None, :], axis=0).reshape(rows, slots_local)
        return (needed, jnp.max(jnp.sum(needed.astype(jnp.int32), axis=1)))

    need_first, load_first = needed_of(first)
    need_last, load_last = needed_of(last)
    use_last = load_last < load_first
    source = jnp.where(use_last, last, first)
    needed = jnp.where(use_last, need_last, need_first)
    load = jnp.minimum(load_first, load_last)
    rank = jnp.cumsum(needed.astype(jnp.int32), axis=1) - 1
    local_ids = jnp.arange(slots_local, dtype=jnp.int32)
    picks = jnp.stack(
        [jnp.argmax(needed & (rank == k), axis=1).astype(jnp.int32) for k in range(slots_local)],
        axis=1,
    )
    my_picks = picks[ex_index]
    src_dev = source // slots_local
    src_rank = rank.reshape(-1)[source]
    fast = min(2, slots_local)
    spread_a = spread_slots(expert_gate_up, expert_down, my_picks[:fast], ex_count)
    out_a = spread_a[src_dev * fast + jnp.minimum(src_rank, fast - 1)]
    if slots_local > fast:
        rest = slots_local - fast

        def extra():
            spread_b = spread_slots(expert_gate_up, expert_down, my_picks[fast:], ex_count)
            return spread_b[src_dev * rest + jnp.clip(src_rank - fast, 0, rest - 1)]

        out_b = lax.cond(load > fast, extra, lambda: jnp.zeros_like(out_a))
        out_a = jnp.where((src_rank < fast)[:, None, None, None], out_a, out_b)
    arrived = lax.all_to_all(out_a, "expert", split_axis=0, concat_axis=2, tiled=True)
    is_moved = local_ids == moved_slot[ex_index]
    moved_gate_up = jnp.where(is_moved[:, None, None, None], arrived[:, :2], expert_gate_up)
    moved_down = jnp.where(is_moved[:, None, None], arrived[:, 2], expert_down)
    return (moved_gate_up, moved_down)


def local(
    hidden,
    attn_gain,
    query_weight,
    latent_down,
    latent_up,
    out_weight,
    latent_pool,
    page_table,
    page_counts,
    ffn_gain,
    expert_ids,
    expert_gates,
    old_place,
    new_place,
    expert_gate_up,
    expert_down,
    shared_gate_up,
    shared_down,
):
    dp_count = lax.axis_size("dp")
    ex_count = lax.axis_size("expert")
    dp_index = lax.axis_index("dp")
    ex_index = lax.axis_index("expert")
    req_local = hidden.shape[0]
    group_rows = req_local * ex_count
    requests = page_counts.shape[0]
    head_local = query_weight.shape[0] // (NOPE + ROPE)
    score_scale = (NOPE + ROPE) ** (-0.5)
    group_start = dp_index * group_rows
    everyone = gather_rows(hidden)
    normed = rms_norm(everyone.astype(jnp.float32), attn_gain).astype(jnp.bfloat16)
    queries = jnp.einsum(
        "td,qd->tq", normed, query_weight, preferred_element_type=jnp.float32
    ).reshape(requests, head_local, NOPE + ROPE)
    position = (page_counts * PAGE).astype(jnp.float32)
    query_rope = rotary(queries[..., NOPE:], position[:, None]).astype(jnp.bfloat16)
    up_table = latent_up.reshape(LATENT, head_local, NOPE + VHEAD)
    query_latent = jnp.einsum(
        "thn,lhn->thl",
        queries[..., :NOPE],
        up_table[..., :NOPE].astype(jnp.float32),
        precision=HIGHEST,
    ).astype(jnp.bfloat16)
    pages_local = latent_pool.shape[0]
    pool_total = pages_local * dp_count
    flat_pages = page_table.reshape(-1)
    flat_owner = jnp.repeat(jnp.arange(requests, dtype=jnp.int32), page_table.shape[1])
    target = jnp.where(flat_pages >= 0, flat_pages, pool_total)
    owner_all = jnp.full((pool_total,), -1, jnp.int32).at[target].set(flat_owner, mode="drop")
    page_owner = lax.dynamic_slice_in_dim(owner_all, dp_index * pages_local, pages_local)
    page_used = page_owner >= 0
    owner_safe = jnp.maximum(page_owner, 0)
    page_latent = latent_pool[..., :LATENT]
    page_rope = latent_pool[..., LATENT:]
    scores = jnp.einsum(
        "phl,pkl->phk", query_latent[owner_safe], page_latent, preferred_element_type=jnp.float32
    )
    scores = (
        scores
        + jnp.einsum(
            "phr,pkr->phk", query_rope[owner_safe], page_rope, preferred_element_type=jnp.float32
        )
    ) * score_scale
    raw_max = jnp.max(scores, axis=2)
    weights = jnp.exp(scores - raw_max[..., None])
    page_total = jnp.sum(weights, axis=2)
    page_mix = jnp.einsum(
        "phk,pkl->phl",
        weights.astype(jnp.bfloat16),
        page_latent,
        preferred_element_type=jnp.float32,
    )
    page_max = jnp.where(page_used[:, None], raw_max, MASKED_SCORE)
    member = page_owner[None, :] == jnp.arange(requests, dtype=jnp.int32)[:, None]
    req_max = jnp.max(jnp.where(member[:, :, None], page_max[None], MASKED_SCORE), axis=1)
    rescale = jnp.where(page_used[:, None], jnp.exp(page_max - req_max[owner_safe]), 0.0)
    member_float = member.astype(jnp.float32)
    req_total = jnp.dot(member_float, page_total * rescale, precision=HIGHEST)
    req_mix = jnp.einsum(
        "rp,phl->rhl", member_float, page_mix * rescale[..., None], precision=HIGHEST
    )
    packed = jnp.concatenate([req_mix, req_max[..., None], req_total[..., None]], axis=-1)
    gathered = lax.all_gather(packed, "dp", axis=0, tiled=False)
    gathered = lax.dynamic_slice_in_dim(gathered, group_start, group_rows, 1)
    each_max = gathered[..., LATENT]
    part_max = jnp.max(each_max, axis=0)
    each_weight = jnp.exp(each_max - part_max[None])
    part_total = jnp.sum(gathered[..., LATENT + 1] * each_weight, axis=0)
    part_mix = jnp.sum(gathered[..., :LATENT] * each_weight[..., None], axis=0)
    own_normed = lax.dynamic_slice_in_dim(normed, group_start, group_rows, 0)
    own_position = lax.dynamic_slice_in_dim(position, group_start, group_rows, 0)
    fresh_latent = jnp.dot(own_normed, latent_down, preferred_element_type=jnp.float32)
    new_latent = rms_plain(fresh_latent[:, :LATENT]).astype(jnp.bfloat16)
    new_rope = rotary(fresh_latent[:, LATENT:], own_position).astype(jnp.bfloat16)
    own_query = lax.dynamic_slice_in_dim(query_latent, group_start, group_rows, 0)
    own_rope_query = lax.dynamic_slice_in_dim(query_rope, group_start, group_rows, 0)
    own_score = jnp.einsum("thl,tl->th", own_query, new_latent, preferred_element_type=jnp.float32)
    own_score = (
        own_score
        + jnp.einsum("thr,tr->th", own_rope_query, new_rope, preferred_element_type=jnp.float32)
    ) * score_scale
    highest = jnp.maximum(part_max, own_score)
    kept_part = jnp.exp(part_max - highest)
    own_weight = jnp.exp(own_score - highest)
    denominator = part_total * kept_part + own_weight
    numerator = (
        part_mix * kept_part[..., None]
        + own_weight[..., None] * new_latent.astype(jnp.float32)[:, None, :]
    )
    attended = (numerator / denominator[..., None]).astype(jnp.bfloat16)
    heads_out = jnp.einsum(
        "thl,lhv->thv", attended, up_table[..., NOPE:], preferred_element_type=jnp.float32
    )
    heads_out = heads_out.astype(jnp.bfloat16).reshape(group_rows, head_local * VHEAD)
    partial_value = jnp.dot(heads_out, out_weight, preferred_element_type=jnp.float32)
    attn_out = lax.psum_scatter(partial_value, "expert", scatter_dimension=0, tiled=True)
    residual = hidden.astype(jnp.float32) + attn_out
    normed_ffn = rms_norm(residual, ffn_gain).astype(jnp.bfloat16)
    slots_local = expert_gate_up.shape[0]
    ff_width = expert_gate_up.shape[2]
    col_width = expert_gate_up.shape[3]
    every_row = gather_rows(normed_ffn)
    my_columns = lax.dynamic_slice_in_dim(every_row, dp_index * col_width, col_width, 1)
    by_group = my_columns.reshape(dp_count, ex_count, req_local, col_width).transpose(1, 0, 2, 3)
    ffn_rows = by_group.reshape(requests, col_width)
    column_rows = lax.dynamic_index_in_dim(by_group, ex_index, 0, keepdims=False).reshape(
        dp_count * req_local, col_width
    )
    top_count = expert_ids.shape[1]
    experts_count = EXP_DEV * ex_count
    ids_order = (
        expert_ids.reshape(dp_count, ex_count, req_local, top_count)
        .transpose(1, 0, 2, 3)
        .reshape(requests, top_count)
    )
    gates_order = (
        expert_gates.reshape(dp_count, ex_count, req_local, top_count)
        .transpose(1, 0, 2, 3)
        .reshape(requests, top_count)
    )
    old_flat = old_place.reshape(-1)
    holds_map = old_flat[None, :] == jnp.arange(experts_count, dtype=jnp.int32)[:, None]
    holder = jnp.argmax(holds_map, axis=1)
    slot_of = holder[ids_order.reshape(-1)]
    capacity = 2 * requests * top_count // experts_count
    local_slot = slot_of - ex_index * slots_local
    slot_hot = local_slot[:, None] == jnp.arange(slots_local, dtype=jnp.int32)[None, :]
    slot_rank = jnp.cumsum(slot_hot.astype(jnp.int32), axis=0) - 1
    position_in = jnp.where(slot_hot, slot_rank, capacity)
    route_hot = (
        position_in[:, :, None] == jnp.arange(capacity, dtype=jnp.int32)[None, None, :]
    ).astype(jnp.float32)
    route_hot = route_hot.reshape(requests, top_count, slots_local, capacity)
    dispatch = jnp.sum(route_hot, axis=1).astype(jnp.bfloat16)
    combine = jnp.sum(route_hot * gates_order[:, :, None, None], axis=1)
    slot_inputs = jnp.einsum(
        "tsc,td->scd", dispatch, ffn_rows, preferred_element_type=jnp.float32
    ).astype(jnp.bfloat16)
    routed_part = jnp.einsum(
        "scd,sgfd->sgcf", slot_inputs, expert_gate_up, preferred_element_type=jnp.float32
    )
    shared_part = jnp.einsum(
        "td,gfd->gtf", column_rows, shared_gate_up, preferred_element_type=jnp.float32
    )
    routed_sum, shared_sum = lax.psum((routed_part, shared_part), "dp")
    activated = (jax.nn.silu(routed_sum[:, 0]) * routed_sum[:, 1]).astype(jnp.bfloat16)
    slot_out = jnp.einsum(
        "scf,sfd->scd", activated, expert_down, preferred_element_type=jnp.float32
    )
    routed = jnp.einsum("tsc,scd->td", combine, slot_out, precision=HIGHEST)
    shared_act = (jax.nn.silu(shared_sum[0]) * shared_sum[1]).astype(jnp.bfloat16)
    shared_term = jnp.dot(shared_act, shared_down, preferred_element_type=jnp.float32)
    moe_rows = lax.psum_scatter(routed, "expert", scatter_dimension=0, tiled=True)
    moe_part = lax.all_to_all(moe_rows + shared_term, "dp", split_axis=0, concat_axis=1, tiled=True)
    layer_out = (residual + moe_part).astype(jnp.bfloat16)
    moved_gate_up, moved_down = migrate(expert_gate_up, expert_down, old_place, new_place, ex_index)
    return (layer_out, moved_gate_up, moved_down)


def solution(mesh):
    in_specs = (
        P(("dp", "expert"), None),
        P(),
        P("expert", None),
        P(),
        P(None, "expert"),
        P("expert", None),
        P("dp", None, None),
        P(),
        P(),
        P(),
        P(),
        P(),
        P(),
        P(),
        P("expert", None, None, "dp"),
        P("expert", None, "dp"),
        P(None, None, "dp"),
        P(None, "dp"),
    )
    out_specs = (P(("dp", "expert"), None), P("expert", None, None, "dp"), P("expert", None, "dp"))
    return jax.shard_map(local, mesh=mesh, in_specs=in_specs, out_specs=out_specs, check_vma=False)
```

profile of v0, /device:TPU:0, one launch (start us, length us, event | category | flops | bytes accessed | tf_op | source)
XLA Modules:
  0.0 691.7 jit_solution(8807751896408755276)
XLA Ops:
  18.1 5.9 mini-gather-slice.2
  24.0 5.2 mini-gather-slice.3
  30.6 5.2 gather_fusion.11
  35.8 4.7 gather_fusion.12
  40.5 5.0 gather_fusion.8
  45.5 5.6 pad_maximum_fusion.3
  51.1 7.7 %pad_maximum_fusion.2 = bf16[2,3,8,176,512]{4,3,2,1,0:T(8,128)(2,1)} fusion(bf16[2,1,8,176,512]{4,3,2,1,0:T(8,128)(2,1)} %bitcast.229, bf16[2,2,8,176,512]{4,3,2,1,0:T(8,128)(2,1)} %bitcast.225), kind=kLoop, calls=%fused_computation.22 | loop fusion | flops 4325376 | bytes 17301504 | tf_op jit(solution)/shard_map/concatenate | solution.py:49
  58.8 7.6 %copy.166 = bf16[2,3,8,176,512]{4,3,1,0,2:T(8,128)(2,1)} copy(bf16[2,3,8,176,512]{4,3,2,1,0:T(8,128)(2,1)} %pad_maximum_fusion.2) | data formatting | bytes 17301504 | tf_op jit(solution)/shard_map/concatenate | solution.py:49
  68.7 2.5 conditional.1
  71.3 6.5 all-to-all-start.2
  77.8 195.6 %all-gather.1 = bf16[8,1,2048]{2,1,0:T(2,128)(2,1)S(1)} all-gather(bf16[1,1,2048]{2,1,0:T(2,128)(2,1)S(1)} %bitcast.240), channel_id=1, replica_groups=mesh['dp'=4,'expert'=8] {'expert'}, dimensions={0}, use_global_device_ids=true | all-gather | bytes 36864 | tf_op jit(solution)/shard_map/all_gather | solution.py:44
  273.4 8.5 %all_gather.19 = bf16[32,2048]{1,0:T(8,128)(2,1)S(1)} all-gather(bf16[8,2048]{1,0:T(8,128)(2,1)S(1)} %bitcast.236), channel_id=1, replica_groups=mesh['dp'=4,'expert'=8] {'dp'}, dimensions={0}, use_global_device_ids=true | all-gather | bytes 163840 | tf_op jit(solution)/shard_map/all_gather | solution.py:45
  289.1 2.6 scatter_custom_fusion
  320.0 11.4 %all-gather = f32[128,2,514]{2,0,1:T(8,128)S(1)} all-gather(f32[32,2,514]{2,0,1:T(8,128)S(1)} %pad_maximum_fusion.4), channel_id=2, replica_groups=mesh['dp'=4,'expert'=8] {'dp'}, dimensions={0}, use_global_device_ids=true | all-gather | bytes 657920 | tf_op jit(solution)/shard_map/all_gather | solution.py:190
  345.4 3.0 multiply_reduce_fusion
  354.8 4.5 compare_select_fusion.5
  359.4 10.5 %select_subtract_fusion = s32[192]{0:T(256)S(1)} fusion(pred[192]{0:T(512)(128)(4,1)S(1)} %get-tuple-element.86, pred[192]{0:T(512)(128)(4,1)S(1)} %get-tuple-element.85, pred[192]{0:T(512)(128)(4,1)S(1)} %get-tuple-element.84, pred[192]{0:T(512)(128)(4,1)S(1)} %get-tuple-element.83, pred[192]{0:T(512)(128)(4,1)S(1)} %get-tuple-element.82, ...), kind=kLoop, calls=%fused_computation.212 | loop fusion | flops 3456 | bytes 4872 | tf_op jit(solution)/shard_map/sub | solution.py:253
  372.7 32.9 %all-reduce.8.cloned.1.call-done = f32[8,2048]{1,0:T(8,128)} async-done(((f32[8,2048]{1,0:T(8,128)}), f32[8,2048]{1,0:T(8,128)}) %all-reduce.8.cloned.1.call-update) | async-done | bytes 65552
  408.4 14.0 %all-gather.2 = bf16[8,1,2048]{2,1,0:T(2,128)(2,1)S(1)} all-gather(bf16[1,1,2048]{2,1,0:T(2,128)(2,1)S(1)} %convert_bitcast_fusion), channel_id=1, replica_groups=mesh['dp'=4,'expert'=8] {'expert'}, dimensions={0}, use_global_device_ids=true | all-gather | bytes 36864 | tf_op jit(solution)/shard_map/all_gather | solution.py:44
  422.4 8.4 %all_gather.23 = bf16[32,2048]{1,0:T(8,128)(2,1)S(1)} all-gather(bf16[8,2048]{1,0:T(8,128)(2,1)S(1)} %bitcast.237), channel_id=1, replica_groups=mesh['dp'=4,'expert'=8] {'dp'}, dimensions={0}, use_global_device_ids=true | all-gather | bytes 163840 | tf_op jit(solution)/shard_map/all_gather | solution.py:45
  430.9 4.9 convolution_bitcast_fusion
  435.8 6.9 convolution_bitcast_fusion.1
  443.4 46.9 %all-reduce.12.cloned.1.call-done = (f32[2,4,2816]{2,1,0:T(4,128)}, f32[4,2,16,1408]{3,2,1,0:T(8,128)}) async-done(((f32[2,4,2816]{2,1,0:T(4,128)}, f32[4,2,16,1408]{3,2,1,0:T(8,128)}), (f32[2,4,2816]{2,1,0:T(4,128)}, f32[4,2,16,1408]{3,2,1,0:T(8,128)})) %all-reduce.12.cloned.1.call-update) | async-done | bytes 811024 | tf_op jit(solution)/shard_map/psum | solution.py:272
  490.3 3.8 fusion.18
  495.6 53.2 %all-reduce.10.cloned.1.call-done = f32[32,512]{1,0:T(8,128)} async-done(((f32[32,512]{1,0:T(8,128)}), f32[32,512]{1,0:T(8,128)}) %all-reduce.10.cloned.1.call-update) | async-done | bytes 65552
  550.6 3.6 all-to-all-start.1
  554.3 6.3 gather_fusion.9
  560.6 6.1 broadcast_select_fusion.2
  566.7 4.6 all-to-all-start.3
  573.1 95.0 %all-to-all-done.3 = bf16[8,3,176,512]{3,2,1,0:T(8,128)(2,1)} async-done(((bf16[8,3,176,512]{3,2,1,0:T(8,128)(2,1)}), bf16[8,3,176,512]{3,2,1,0:T(8,128)(2,1)}, u32[]{:S(2)}, u32[]{:S(2)}) %all-to-all-start.3) | async-done | bytes 4325408 | tf_op jit(solution)/shard_map/all_to_all | solution.py:100
  670.9 11.0 %broadcast_select_fusion = bf16[4,2,1408,512]{3,2,1,0:T(8,128)(2,1)} fusion(bf16[4,2,1408,512]{3,2,1,0:T(8,128)(2,1)} %param.34, pred[4]{0:T(512)(128)(4,1)S(1)} %iota_compare_fusion.9, bf16[2,1408,512]{2,1,0:T(8,128)(2,1)S(1)} %slice_bitcast_fusion), kind=kLoop, calls=%fused_computation.21 | loop fusion | flops 5767168 | bytes 25952260 | tf_op jit(solution)/shard_map/jit(_where)/select_n | solution.py:102
  681.9 3.2 broadcast_select_fusion.1
  (221 shorter events, 83.6 us)
Async XLA Ops:
  7.2 541.6 %copy-start = (bf16[2816,512]{1,0:T(8,128)(2,1)S(1)}, bf16[2816,512]{1,0:T(8,128)(2,1)}, u32[]{:S(2)}) copy-start(bf16[2816,512]{1,0:T(8,128)(2,1)} %param.37) | copy-start | bytes 8650756
  9.3 2.3 copy-start.26
  10.8 1.6 copy-start.19
  71.3 6.5 copy-start.10
  71.3 210.8 %copy-start.16 = (f32[2048]{0:T(1024)S(1)}, f32[2048]{0:T(1024)}, u32[]{:S(2)}) copy-start(f32[2048]{0:T(1024)} %param.21) | copy-start | bytes 24580
  71.3 213.0 %copy-start.17 = (s32[32,16]{0,1:T(8,128)S(1)}, s32[32,16]{0,1:T(8,128)}, u32[]{:S(2)}) copy-start(s32[32,16]{0,1:T(8,128)} %param.27) | copy-start | bytes 6148
  71.3 479.3 %all-to-all-start.2 = ((bf16[2,3,8,176,512]{4,3,1,0,2:T(8,128)(2,1)}), bf16[2,3,8,176,512]{4,3,1,0,2:T(8,128)(2,1)}, u32[]{:S(2)}, u32[]{:S(2)}) async-start(bf16[2,3,8,176,512]{4,3,1,0,2:T(8,128)(2,1)} %copy.166), calls=%async_computation.2 | async-start | bytes 17301504 | tf_op jit(solution)/shard_map/all_to_all | solution.py:52
  77.7 327.9 %all-reduce.8.cloned.1.call-start = ((), (), s32[]{:S(2)}) async-start(), calls=%async_computation.4 | async-start | bytes 131072
  286.8 55.8 %copy-start.1 = (bf16[512,512]{0,1:T(8,128)(2,1)}, bf16[512,512]{0,1:T(8,128)(2,1)S(1)}, u32[]{:S(2)}) copy-start(bf16[512,512]{0,1:T(8,128)(2,1)S(1)} %copy.145) | copy-start | bytes 1572868
  287.8 0.6 copy-start.4
  291.7 2.0 copy-start.23
  302.9 3.3 copy-start.6
  331.3 0.8 copy-start.2
  332.9 12.5 %copy-start.13 = (f32[8,2]{0,1:T(2,128)}, f32[8,2]{0,1:T(2,128)S(1)}, u32[]{:S(2)}) copy-start(f32[8,2]{0,1:T(2,128)S(1)} %get-tuple-element.98) | copy-start | bytes 196
  333.8 11.6 %copy-start.9 = (f32[4,8,2,1]{1,0,3,2:T(4,128)}, f32[4,8,2,1]{1,0,3,2:T(4,128)S(1)}, u32[]{:S(2)}) copy-start(f32[4,8,2,1]{1,0,3,2:T(4,128)S(1)} %copy.182) | copy-start | bytes 772
  337.6 0.6 copy-start.5
  338.2 10.3 %copy-start.14 = (f32[4,8,2,1]{1,0,3,2:T(4,128)S(1)}, f32[4,8,2,1]{1,0,3,2:T(4,128)}, u32[]{:S(2)}) copy-start(f32[4,8,2,1]{1,0,3,2:T(4,128)} %copy.183) | copy-start | bytes 772
  338.2 14.2 %copy-start.21 = (s32[32,6]{0,1:T(8,128)S(1)}, s32[32,6]{0,1:T(8,128)}, u32[]{:S(2)}) copy-start(s32[32,6]{0,1:T(8,128)} %param.30) | copy-start | bytes 2308
  338.2 14.5 %copy-start.20 = (s32[32]{0:T(128)S(1)}, s32[32]{0:T(128)}, u32[]{:S(2)}) copy-start(s32[32]{0:T(128)} %copy-done.19) | copy-start | bytes 388
  338.2 33.5 %copy-start.22 = (f32[32,6]{0,1:T(8,128)S(1)}, f32[32,6]{0,1:T(8,128)}, u32[]{:S(2)}) copy-start(f32[32,6]{0,1:T(8,128)} %param.31) | copy-start | bytes 2308
  338.2 33.8 %copy-start.28 = (u32[32]{0:T(128)S(1)}, u32[32]{0:T(128)}, u32[]{:S(2)}) copy-start(u32[32]{0:T(128)} %constant.206) | copy-start | bytes 388
  338.3 67.3 %copy-start.11 = (bf16[1,2048]{1,0:T(2,128)(2,1)S(1)}, bf16[1,2048]{1,0:T(2,128)(2,1)}, u32[]{:S(2)}) copy-start(bf16[1,2048]{1,0:T(2,128)(2,1)} %param.20) | copy-start | bytes 12292
  338.3 70.1 %copy-start.18 = (f32[2048]{0:T(1024)S(1)}, f32[2048]{0:T(1024)}, u32[]{:S(2)}) copy-start(f32[2048]{0:T(1024)} %param.29) | copy-start | bytes 24580
  352.4 137.9 %all-reduce.12.cloned.1.call-start = ((), (), s32[]{:S(2)}) async-start(), calls=%async_computation.6 | async-start | bytes 1622016 | tf_op jit(solution)/shard_map/psum | solution.py:272
  442.7 106.1 %all-reduce.10.cloned.1.call-start = ((), (), s32[]{:S(2)}) async-start(), calls=%async_computation.5 | async-start | bytes 131072
  490.3 4.7 copy-start.24
  490.3 58.5 %copy-start.12 = (f32[2,4,2816]{2,1,0:T(4,128)S(1)}, f32[2,4,2816]{2,1,0:T(4,128)}, u32[]{:S(2)}) copy-start(f32[2,4,2816]{2,1,0:T(4,128)} %get-tuple-element.87) | copy-start | bytes 270340
  550.6 16.1 %all-to-all-start.1 = ((f32[4,1,512]{2,1,0:T(1,128)}), f32[4,1,512]{2,1,0:T(1,128)S(1)}, u32[]{:S(2)}, u32[]{:S(2)}) async-start(f32[4,1,512]{2,1,0:T(1,128)} %copy.164), calls=%async_computation.1 | async-start | bytes 16384 | tf_op jit(solution)/shard_map/all_to_all | solution.py:281
  566.7 4.6 copy-start.27
  566.7 101.4 %all-to-all-start.3 = ((bf16[8,3,176,512]{3,2,1,0:T(8,128)(2,1)}), bf16[8,3,176,512]{3,2,1,0:T(8,128)(2,1)}, u32[]{:S(2)}, u32[]{:S(2)}) async-start(bf16[8,3,176,512]{3,2,1,0:T(8,128)(2,1)} %broadcast_select_fusion.2), calls=%async_computation.3 | async-start | bytes 8650752 | tf_op jit(solution)/shard_map/all_to_all | solution.py:100
  670.6 11.3 %slice-start = ((s8[5767168]{0:T(1024)(128)(4,1)}), s8[4194304]{0:T(1024)(128)(4,1)S(1)}, s32[]{:S(2)}) async-start(s8[5767168]{0:T(1024)(128)(4,1)} %bitcast.223), calls=%async_computation.7 | async-start | bytes 8388608
  670.9 11.0 %slice-start.1 = ((s8[5767168]{0:T(1024)(128)(4,1)}), s8[1572864]{0:T(1024)(128)(4,1)S(1)}, s32[]{:S(2)}) async-start(s8[5767168]{0:T(1024)(128)(4,1)} %bitcast.223), calls=%async_computation.8 | async-start | bytes 3145728
  (5 other events, 3.0 us)
Sparse Core Ops, SparseCore 0:
  352.5 53.0 all-reduce.7
  442.8 47.3 all-reduce.11
  495.1 53.6 all-reduce.9
where the time goes:
time: 694 us; the launch traced here: 692 us
  blocking collectives  238 us (34%)
  waiting for transfers between devices  228 us (33%)
  local copies, waits for them, and re-layouts  79.7 us (11%)
  other arithmetic  79.7 us (11%)
  matrix products  33.6 us (5%)
  between operations  18.1 us (3%)
  starting transfers between devices  14.8 us (2%)
    all_gather x2, blocking collectives, gather_rows(): by_expert = lax.all_gather(rows, 'expert', axis=0, tiled=True)  210 us
    all_to_all x1, waiting for transfers between devices, migrate(): lax.all_to_all(out_a, 'expert', split_axis=0, concat_axis=2, tiled=True)  95 us
    unnamed x5, waiting for transfers between devices  86.2 us
    psum x1, waiting for transfers between devices, local(): routed_sum, shared_sum = lax.psum((routed_part, shared_part), 'dp')  46.9 us
    gather x5, local copies, waits for them, and re-layouts, spread_slots(): chosen = jnp.concatenate([gate_up[picks], down[picks][:, None]], axis=1)  25.9 us
    all_gather x2, blocking collectives, gather_rows(): return lax.all_gather(by_expert, 'dp', axis=0, tiled=True)  16.9 us
  transfers between devices with their start and end apart: 6, of which 4 were waited for; matrix products, arithmetic and copies ran while one was open for 16% of the time, Pallas kernels for 0%

commit v1 on v0

--- a/solution.py
+++ b/solution.py
@@ -14,6 +14,17 @@
 ROPE_BASE = 50000.0
 MASKED_SCORE = -1e30
 HIGHEST = lax.Precision.HIGHEST
+
+
+def around_the_ring(x, name, dim):
+    size = lax.axis_size(name)
+    right = [(i, (i + 1) % size) for i in range(size)]
+    blocks = [x]
+    for reach in range(1, size):
+        blocks = [lax.ppermute(blocks[0], name, right), *blocks]
+    whole = jnp.concatenate(blocks, axis=dim)
+    shift = (lax.axis_index(name) + 1) * blocks[-1].shape[dim]
+    return jnp.roll(whole, shift, axis=dim)
 
 
 def rms_plain(values):
@@ -41,7 +52,7 @@
 
 
 def gather_rows(rows):
-    by_expert = lax.all_gather(rows, "expert", axis=0, tiled=True)
+    by_expert = around_the_ring(rows, "expert", 0)
     return lax.all_gather(by_expert, "dp", axis=0, tiled=True)
 
 

time: 694 us -> 721 us (1.039)
  blocking collectives: 238 us -> 28.3 us
  waiting for transfers between devices: 228 us -> 425 us
  starting transfers between devices: 14.8 us -> 54.5 us
    all_gather x2 -> x0, blocking collectives: 210 us -> none  [gather_rows(): by_expert = lax.all_gather(rows, 'expert', axis=0, tiled=True)]
    ppermute x0 -> x14, waiting for transfers between devices: none -> 182 us  [around_the_ring(): blocks = [lax.ppermute(blocks[0], name, right), *blocks]]
    ppermute x0 -> x14, starting transfers between devices: none -> 39.7 us  [around_the_ring(): blocks = [lax.ppermute(blocks[0], name, right), *blocks]]
    unnamed x5, waiting for transfers between devices: 86.2 us -> 101 us
  transfers between devices with their start and end apart: 6 -> 20, of which waited for: 4 -> 17; matrix products, arithmetic and copies ran while one was open for 16% -> 16% of each run, Pallas kernels for 0% -> 0%
where the time goes in v1:
time: 721 us; the launch traced here: 718 us
  waiting for transfers between devices  425 us (59%)
  local copies, waits for them, and re-layouts  79.9 us (11%)
  other arithmetic  79.1 us (11%)
  starting transfers between devices  54.5 us (8%)
  matrix products  33.4 us (5%)
  blocking collectives  28.3 us (4%)
  between operations  18.3 us (3%)
    ppermute x14, waiting for transfers between devices, around_the_ring(): blocks = [lax.ppermute(blocks[0], name, right), *blocks]  182 us
    unnamed x5, waiting for transfers between devices  101 us
    all_to_all x1, waiting for transfers between devices, migrate(): lax.all_to_all(out_a, 'expert', split_axis=0, concat_axis=2, tiled=True)  95 us
    psum x1, waiting for transfers between devices, local(): routed_sum, shared_sum = lax.psum((routed_part, shared_part), 'dp')  46.1 us
    ppermute x14, starting transfers between devices, around_the_ring(): blocks = [lax.ppermute(blocks[0], name, right), *blocks]  39.7 us
    gather x5, local copies, waits for them, and re-layouts, spread_slots(): chosen = jnp.concatenate([gate_up[picks], down[picks][:, None]], axis=1)  25.9 us
    all_gather x2, blocking collectives, gather_rows(): return lax.all_gather(by_expert, 'dp', axis=0, tiled=True)  17.1 us
  transfers between devices with their start and end apart: 20, of which 17 were waited for; matrix products, arithmetic and copies ran while one was open for 16% of the time, Pallas kernels for 0%

profile of v1, /device:TPU:0, one launch (start us, length us, event | category | flops | bytes accessed | tf_op | source)
XLA Modules:
  0.0 718.4 jit_solution(5115303230846686890)
XLA Ops:
  18.3 5.9 mini-gather-slice.2
  24.2 5.2 mini-gather-slice.3
  30.9 5.2 gather_fusion.11
  36.1 4.7 gather_fusion.12
  40.8 5.0 gather_fusion.8
  45.8 5.6 pad_maximum_fusion.3
  51.4 7.7 %pad_maximum_fusion.2 = bf16[2,3,8,176,512]{4,3,2,1,0:T(8,128)(2,1)} fusion(bf16[2,1,8,176,512]{4,3,2,1,0:T(8,128)(2,1)} %bitcast.220, bf16[2,2,8,176,512]{4,3,2,1,0:T(8,128)(2,1)} %bitcast.216), kind=kLoop, calls=%fused_computation.22 | loop fusion | flops 4325376 | bytes 17301504 | tf_op jit(solution)/shard_map/concatenate | solution.py:60
  59.1 7.6 %copy.166 = bf16[2,3,8,176,512]{4,3,1,0,2:T(8,128)(2,1)} copy(bf16[2,3,8,176,512]{4,3,2,1,0:T(8,128)(2,1)} %pad_maximum_fusion.2) | data formatting | bytes 17301504 | tf_op jit(solution)/shard_map/concatenate | solution.py:60
  71.6 6.5 all-to-all-start.2
  82.7 139.2 %collective-permute-done = bf16[1,2048]{1,0:T(2,128)(2,1)S(1)} collective-permute-done((bf16[1,2048]{1,0:T(2,128)(2,1)S(1)}, bf16[1,2048]{1,0:T(2,128)(2,1)S(1)}, u32[]{:S(2)}, u32[]{:S(2)}) %collective-permute-start) | collective-permute-done | bytes 4128 | tf_op jit(solution)/shard_map/ppermute | solution.py:24
  222.6 4.3 collective-permute-done.1
  227.5 4.4 collective-permute-done.2
  231.9 36.1 %collective-permute-start.3 = (bf16[1,2048]{1,0:T(2,128)(2,1)S(1)}, bf16[1,2048]{1,0:T(2,128)(2,1)S(1)}, u32[]{:S(2)}, u32[]{:S(2)}) collective-permute-start(bf16[1,2048]{1,0:T(2,128)(2,1)S(1)} %collective-permute-done.2), channel_id=1, source_target_pairs={{0,1},{1,2},{2,3},{3,4},{4,5},{5,6},{6,7},{7,0},{8,9},{9,10},{10,1... | collective-permute-start | bytes 12296 | tf_op jit(solution)/shard_map/ppermute | solution.py:24
  283.6 8.7 %all_gather.12 = bf16[32,2048]{1,0:T(8,128)(2,1)S(1)} all-gather(bf16[8,2048]{1,0:T(8,128)(2,1)S(1)} %fusion.26), channel_id=1, replica_groups=mesh['dp'=4,'expert'=8] {'dp'}, dimensions={0}, use_global_device_ids=true | all-gather | bytes 163840 | tf_op jit(solution)/shard_map/all_gather | solution.py:56
  323.7 11.2 %all-gather = f32[128,2,514]{2,0,1:T(8,128)S(1)} all-gather(f32[32,2,514]{2,0,1:T(8,128)S(1)} %pad_maximum_fusion.4), channel_id=2, replica_groups=mesh['dp'=4,'expert'=8] {'dp'}, dimensions={0}, use_global_device_ids=true | all-gather | bytes 657920 | tf_op jit(solution)/shard_map/all_gather | solution.py:201
  358.9 48.2 %all-reduce.8.cloned.1.call-done = f32[8,2048]{1,0:T(8,128)} async-done(((f32[8,2048]{1,0:T(8,128)}), f32[8,2048]{1,0:T(8,128)}) %all-reduce.8.cloned.1.call-update) | async-done | bytes 65552
  410.0 4.8 collective-permute-done.7
  414.8 10.6 %select_subtract_fusion = s32[192]{0:T(256)S(1)} fusion(pred[192]{0:T(512)(128)(4,1)S(1)} %get-tuple-element.87, pred[192]{0:T(512)(128)(4,1)S(1)} %get-tuple-element.86, pred[192]{0:T(512)(128)(4,1)S(1)} %get-tuple-element.85, pred[192]{0:T(512)(128)(4,1)S(1)} %get-tuple-element.84, pred[192]{0:T(512)(128)(4,1)S(1)} %get-tuple-element.83, ...), kind=kLoop, calls=%fused_computation.216 | loop fusion | flops 3456 | bytes 4872 | tf_op jit(solution)/shard_map/sub | solution.py:264
  425.5 4.8 collective-permute-done.9
  435.3 4.8 collective-permute-done.11
  440.6 4.4 collective-permute-done.12
  445.0 4.8 collective-permute-done.13
  450.0 8.4 %all_gather.15 = bf16[32,2048]{1,0:T(8,128)(2,1)S(1)} all-gather(bf16[8,2048]{1,0:T(8,128)(2,1)S(1)} %fusion.25), channel_id=1, replica_groups=mesh['dp'=4,'expert'=8] {'dp'}, dimensions={0}, use_global_device_ids=true | all-gather | bytes 163840 | tf_op jit(solution)/shard_map/all_gather | solution.py:56
  458.5 4.9 convolution_bitcast_fusion
  463.4 6.9 convolution_bitcast_fusion.1
  470.9 46.1 %all-reduce.12.cloned.1.call-done = (f32[2,4,2816]{2,1,0:T(4,128)}, f32[4,2,16,1408]{3,2,1,0:T(8,128)}) async-done(((f32[2,4,2816]{2,1,0:T(4,128)}, f32[4,2,16,1408]{3,2,1,0:T(8,128)}), (f32[2,4,2816]{2,1,0:T(4,128)}, f32[4,2,16,1408]{3,2,1,0:T(8,128)})) %all-reduce.12.cloned.1.call-update) | async-done | bytes 811024 | tf_op jit(solution)/shard_map/psum | solution.py:283
  522.4 53.1 %all-reduce.10.cloned.1.call-done = f32[32,512]{1,0:T(8,128)} async-done(((f32[32,512]{1,0:T(8,128)}), f32[32,512]{1,0:T(8,128)}) %all-reduce.10.cloned.1.call-update) | async-done | bytes 65552
  581.0 6.3 gather_fusion.9
  587.4 6.1 broadcast_select_fusion.2
  593.5 4.6 all-to-all-start.3
  599.9 95.0 %all-to-all-done.3 = bf16[8,3,176,512]{3,2,1,0:T(8,128)(2,1)} async-done(((bf16[8,3,176,512]{3,2,1,0:T(8,128)(2,1)}), bf16[8,3,176,512]{3,2,1,0:T(8,128)(2,1)}, u32[]{:S(2)}, u32[]{:S(2)}) %all-to-all-start.3) | async-done | bytes 4325408 | tf_op jit(solution)/shard_map/all_to_all | solution.py:111
  697.7 11.0 %broadcast_select_fusion = bf16[4,2,1408,512]{3,2,1,0:T(8,128)(2,1)} fusion(bf16[4,2,1408,512]{3,2,1,0:T(8,128)(2,1)} %param.36, pred[4]{0:T(512)(128)(4,1)S(1)} %iota_compare_fusion.9, bf16[2,1408,512]{2,1,0:T(8,128)(2,1)S(1)} %slice_bitcast_fusion), kind=kLoop, calls=%fused_computation.21 | loop fusion | flops 5767168 | bytes 25952260 | tf_op jit(solution)/shard_map/jit(_where)/select_n | solution.py:113
  (241 shorter events, 120.7 us)
Async XLA Ops:
  7.2 568.4 %copy-start = (bf16[2816,512]{1,0:T(8,128)(2,1)S(1)}, bf16[2816,512]{1,0:T(8,128)(2,1)}, u32[]{:S(2)}) copy-start(bf16[2816,512]{1,0:T(8,128)(2,1)} %param.39) | copy-start | bytes 8650756
  71.6 207.6 %copy-start.17 = (s32[32,6]{0,1:T(8,128)S(1)}, s32[32,6]{0,1:T(8,128)}, u32[]{:S(2)}) copy-start(s32[32,6]{0,1:T(8,128)} %param.32) | copy-start | bytes 2308
  71.6 505.8 %all-to-all-start.2 = ((bf16[2,3,8,176,512]{4,3,1,0,2:T(8,128)(2,1)}), bf16[2,3,8,176,512]{4,3,1,0,2:T(8,128)(2,1)}, u32[]{:S(2)}, u32[]{:S(2)}) async-start(bf16[2,3,8,176,512]{4,3,1,0,2:T(8,128)(2,1)} %copy.166), calls=%async_computation.2 | async-start | bytes 17301504 | tf_op jit(solution)/shard_map/all_to_all | solution.py:63
  78.0 329.0 %all-reduce.8.cloned.1.call-start = ((), (), s32[]{:S(2)}) async-start(), calls=%async_computation.4 | async-start | bytes 131072
  78.1 143.8 %collective-permute-start = (bf16[1,2048]{1,0:T(2,128)(2,1)S(1)}, bf16[1,2048]{1,0:T(2,128)(2,1)S(1)}, u32[]{:S(2)}, u32[]{:S(2)}) collective-permute-start(bf16[1,2048]{1,0:T(2,128)(2,1)S(1)} %copy-done.8), channel_id=1, source_target_pairs={{0,1},{1,2},{2,3},{3,4},{4,5},{5,6},{6,7},{7,0},{8,9},{9,10},{10,1... | collective-permute-start | bytes 12296 | tf_op jit(solution)/shard_map/ppermute | solution.py:24
  78.8 200.4 %copy-start.19 = (f32[32]{0:T(128)}, f32[32]{0:T(128)S(1)}, u32[]{:S(2)}) copy-start(f32[32]{0:T(128)S(1)} %multiply_exponential_fusion) | copy-start | bytes 388
  221.9 5.0 collective-permute-start.1
  222.6 56.6 %copy-start.13 = (s32[32]{0:T(128)}, s32[32]{0:T(128)S(1)}, u32[]{:S(2)}) copy-start(s32[32]{0:T(128)S(1)} %get-tuple-element.102) | copy-start | bytes 388
  226.9 5.0 collective-permute-start.2
  231.9 36.9 %collective-permute-start.3 = (bf16[1,2048]{1,0:T(2,128)(2,1)S(1)}, bf16[1,2048]{1,0:T(2,128)(2,1)S(1)}, u32[]{:S(2)}, u32[]{:S(2)}) collective-permute-start(bf16[1,2048]{1,0:T(2,128)(2,1)S(1)} %collective-permute-done.2), channel_id=1, source_target_pairs={{0,1},{1,2},{2,3},{3,4},{4,5},{5,6},{6,7},{7,0},{8,9},{9,10},{10,1... | collective-permute-start | bytes 12296 | tf_op jit(solution)/shard_map/ppermute | solution.py:24
  268.8 4.9 collective-permute-start.4
  273.7 4.9 collective-permute-start.5
  278.6 4.9 collective-permute-start.6
  281.3 56.1 %copy-start.1 = (bf16[512,512]{0,1:T(8,128)(2,1)}, bf16[512,512]{0,1:T(8,128)(2,1)S(1)}, u32[]{:S(2)}) copy-start(bf16[512,512]{0,1:T(8,128)(2,1)S(1)} %copy.145) | copy-start | bytes 1572868
  341.2 12.7 %copy-start.16 = (s32[192,1]{0,1:T(1,128)S(1)}, s32[192,1]{0,1:T(1,128)}, u32[]{:S(2)}) copy-start(s32[192,1]{0,1:T(1,128)} %reshape_reshape.3) | copy-start | bytes 2308
  341.2 17.1 %copy-start.24 = (u32[32]{0:T(128)S(1)}, u32[32]{0:T(128)}, u32[]{:S(2)}) copy-start(u32[32]{0:T(128)} %constant.224) | copy-start | bytes 388
  341.2 65.8 %copy-start.9 = (bf16[1,2048]{1,0:T(2,128)(2,1)S(1)}, bf16[1,2048]{1,0:T(2,128)(2,1)}, u32[]{:S(2)}) copy-start(bf16[1,2048]{1,0:T(2,128)(2,1)} %param.22) | copy-start | bytes 12292
  341.3 68.6 %copy-start.15 = (f32[2048]{0:T(1024)S(1)}, f32[2048]{0:T(1024)}, u32[]{:S(2)}) copy-start(f32[2048]{0:T(1024)} %param.31) | copy-start | bytes 24580
  341.3 99.1 %copy-start.18 = (f32[32,6]{0,1:T(8,128)S(1)}, f32[32,6]{0,1:T(8,128)}, u32[]{:S(2)}) copy-start(f32[32,6]{0,1:T(8,128)} %param.33) | copy-start | bytes 2308
  353.9 163.1 %all-reduce.12.cloned.1.call-start = ((), (), s32[]{:S(2)}) async-start(), calls=%async_computation.6 | async-start | bytes 1622016 | tf_op jit(solution)/shard_map/psum | solution.py:283
  409.9 4.9 collective-permute-start.7
  414.8 10.6 %collective-permute-start.8 = (bf16[1,2048]{1,0:T(2,128)(2,1)S(1)}, bf16[1,2048]{1,0:T(2,128)(2,1)S(1)}, u32[]{:S(2)}, u32[]{:S(2)}) collective-permute-start(bf16[1,2048]{1,0:T(2,128)(2,1)S(1)} %collective-permute-done.7), channel_id=1, source_target_pairs={{0,1},{1,2},{2,3},{3,4},{4,5},{5,6},{6,7},{7,0},{8,9},{9,10},{10,1... | collective-permute-start | bytes 12296 | tf_op jit(solution)/shard_map/ppermute | solution.py:24
  425.4 4.9 collective-permute-start.9
  430.4 4.9 collective-permute-start.10
  435.2 4.9 collective-permute-start.11
  440.1 4.9 collective-permute-start.12
  445.0 4.9 collective-permute-start.13
  470.3 105.3 %all-reduce.10.cloned.1.call-start = ((), (), s32[]{:S(2)}) async-start(), calls=%async_computation.5 | async-start | bytes 131072
  517.0 58.5 %copy-start.10 = (f32[2,4,2816]{2,1,0:T(4,128)S(1)}, f32[2,4,2816]{2,1,0:T(4,128)}, u32[]{:S(2)}) copy-start(f32[2,4,2816]{2,1,0:T(4,128)} %get-tuple-element.88) | copy-start | bytes 270340
  577.4 16.1 %all-to-all-start.1 = ((f32[4,1,512]{2,1,0:T(1,128)}), f32[4,1,512]{2,1,0:T(1,128)S(1)}, u32[]{:S(2)}, u32[]{:S(2)}) async-start(f32[4,1,512]{2,1,0:T(1,128)} %copy.164), calls=%async_computation.1 | async-start | bytes 16384 | tf_op jit(solution)/shard_map/all_to_all | solution.py:292
  593.5 101.4 %all-to-all-start.3 = ((bf16[8,3,176,512]{3,2,1,0:T(8,128)(2,1)}), bf16[8,3,176,512]{3,2,1,0:T(8,128)(2,1)}, u32[]{:S(2)}, u32[]{:S(2)}) async-start(bf16[8,3,176,512]{3,2,1,0:T(8,128)(2,1)} %broadcast_select_fusion.2), calls=%async_computation.3 | async-start | bytes 8650752 | tf_op jit(solution)/shard_map/all_to_all | solution.py:111
  697.3 11.3 %slice-start = ((s8[5767168]{0:T(1024)(128)(4,1)}), s8[4194304]{0:T(1024)(128)(4,1)S(1)}, s32[]{:S(2)}) async-start(s8[5767168]{0:T(1024)(128)(4,1)} %bitcast.214), calls=%async_computation.7 | async-start | bytes 8388608
  (15 other events, 76.7 us)
Sparse Core Ops, SparseCore 0:
  354.0 52.9 all-reduce.7
  470.4 46.6 all-reduce.11
  521.8 53.6 all-reduce.9
